TPU v7x, 32 devices: a whole 2x2x4 slice. The times are simulated.
32 devices in a mesh: region: 2 (over y), tile: 4 (over z), corner: 2 (over x), kern: 2 (over core).
Axes of the slice: x: 2, y: 2, z: 4, core: 2. Of those that a mesh axis runs over, the one named last changes fastest.
Arguments:
- tile_mask: bfloat16 [16, 256, 256], P(('region', 'tile')), parts along dimension 0, may hold values from -1 to 1
- master_mask: bfloat16 [8, 256, 256], P(('region', 'tile')), parts along dimension 0, may hold values from -1 to 1
- target: bfloat16 [16, 256, 256], P(('region', 'tile')), parts along dimension 0, may hold values from 0 to 1
- inst_master: int32 [16], P(('region', 'tile')), parts along dimension 0, may hold values from 0 to 3, as said below
- inst_shift: int32 [16, 2], P(('region', 'tile')), parts along dimension 0, may hold values from 0 to 255
- kernels: float32 [2, 12, 2, 32, 32], P('corner'), may hold values from -24 to 24
- kernel_weight: float32 [2, 12], P('corner'), may hold values from 0.05 to 1
- corner_dose: float32 [2], P('corner'), may hold values from 0.6 to 1.6
Outputs:
- tile_grad: float32 [16, 256, 256], P(('region', 'tile')), parts along dimension 0
- master_grad: float32 [8, 256, 256], P(('region', 'tile')), parts along dimension 0
There are 2 independent parts, one for each index of `region`. A program takes and returns all parts, laid end to end along the dimension named above; an argument that names none is the same for every part. Nothing has to cross between parts.
Inputs may be any that keep to these rules, and one draw needn't show every extreme that they name: `inst_master`: each master cell is placed in exactly 2 tiles.
All inputs are finite; a program needn't handle non-finite values.
Results may differ from a plain program's by a relative error of at most 0.0003.
Values may be sent and summed in bfloat16 or wider, within the bound.
No kernel may reach another device: no remote copies, remote signals or barrier semaphores. Data moves between devices by JAX's collectives and lax.ppermute only.
A program may use at most 64 MiB of HBM per device.

v0:
```python
import math
import jax
import jax.numpy as jnp
from jax import lax
from jax.sharding import PartitionSpec as P

P_SIZE = 256
B = 32
precise = lax.Precision.HIGHEST
steepness = 3.0
threshold = 1.0


def band_tables():
    freq = jnp.arange(B, dtype=jnp.int32) - B // 2
    pixel = jnp.arange(P_SIZE, dtype=jnp.int32)
    angle = (
        2.0 * math.pi / P_SIZE * jnp.mod(freq[:, None] * pixel[None, :], P_SIZE).astype(jnp.float32)
    )
    return (jnp.cos(angle), -jnp.sin(angle))


def phase_ramp(shift):
    freq = jnp.arange(B, dtype=jnp.int32) - B // 2
    total = (
        freq[None, :, None] * shift[:, 0][:, None, None]
        + freq[None, None, :] * shift[:, 1][:, None, None]
    )
    angle = 2.0 * math.pi / P_SIZE * jnp.mod(total, P_SIZE).astype(jnp.float32)
    return (jnp.cos(angle), -jnp.sin(angle))


def spectra(masks, cos_tab, sin_tab):
    rows_re = jnp.einsum("bx,nxy->nby", cos_tab, masks, precision=precise)
    rows_im = jnp.einsum("bx,nxy->nby", sin_tab, masks, precision=precise)
    spec_re = jnp.einsum("nby,cy->nbc", rows_re, cos_tab, precision=precise) - jnp.einsum(
        "nby,cy->nbc", rows_im, sin_tab, precision=precise
    )
    spec_im = jnp.einsum("nby,cy->nbc", rows_re, sin_tab, precision=precise) + jnp.einsum(
        "nby,cy->nbc", rows_im, cos_tab, precision=precise
    )
    return (spec_re, spec_im)


def to_field(x_re, x_im, cos_tab, sin_tab, scale):
    half_re = jnp.einsum("bx,nbc->nxc", cos_tab, x_re, precision=precise) + jnp.einsum(
        "bx,nbc->nxc", sin_tab, x_im, precision=precise
    )
    half_im = jnp.einsum("bx,nbc->nxc", cos_tab, x_im, precision=precise) - jnp.einsum(
        "bx,nbc->nxc", sin_tab, x_re, precision=precise
    )
    out_re = (
        jnp.einsum("nxc,cy->nxy", half_re, cos_tab, precision=precise)
        + jnp.einsum("nxc,cy->nxy", half_im, sin_tab, precision=precise)
    ) * scale
    out_im = (
        jnp.einsum("nxc,cy->nxy", half_im, cos_tab, precision=precise)
        - jnp.einsum("nxc,cy->nxy", half_re, sin_tab, precision=precise)
    ) * scale
    return (out_re, out_im)


def back_pixels(x_re, x_im, cos_tab, sin_tab):
    half_re = jnp.einsum("bx,nbc->nxc", cos_tab, x_re, precision=precise) + jnp.einsum(
        "bx,nbc->nxc", sin_tab, x_im, precision=precise
    )
    half_im = jnp.einsum("bx,nbc->nxc", cos_tab, x_im, precision=precise) - jnp.einsum(
        "bx,nbc->nxc", sin_tab, x_re, precision=precise
    )
    return jnp.einsum("nxc,cy->nxy", half_re, cos_tab, precision=precise) + jnp.einsum(
        "nxc,cy->nxy", half_im, sin_tab, precision=precise
    )


def adjoint(g_re, g_im, cos_tab, sin_tab, scale):
    mid_re = jnp.einsum("bx,nxy->nby", cos_tab, g_re, precision=precise) - jnp.einsum(
        "bx,nxy->nby", sin_tab, g_im, precision=precise
    )
    mid_im = jnp.einsum("bx,nxy->nby", cos_tab, g_im, precision=precise) + jnp.einsum(
        "bx,nxy->nby", sin_tab, g_re, precision=precise
    )
    out_re = (
        jnp.einsum("nby,cy->nbc", mid_re, cos_tab, precision=precise)
        - jnp.einsum("nby,cy->nbc", mid_im, sin_tab, precision=precise)
    ) * scale
    out_im = (
        jnp.einsum("nby,cy->nbc", mid_re, sin_tab, precision=precise)
        + jnp.einsum("nby,cy->nbc", mid_im, cos_tab, precision=precise)
    ) * scale
    return (out_re, out_im)


def on_device(
    tile_mask, master_mask, target, inst_master, inst_shift, kernels, kernel_weight, corner_dose
):
    cos_tab, sin_tab = band_tables()
    scale = 1.0 / (P_SIZE * P_SIZE)
    local_tiles = tile_mask.shape[0]
    tile_re, tile_im = spectra(tile_mask.astype(jnp.float32), cos_tab, sin_tab)
    ph_re, ph_im = phase_ramp(inst_shift)

    def picker(count):
        index = jnp.arange(count, dtype=jnp.int32)
        return (inst_master[:, None] == index[None, :]).astype(jnp.float32)

    piece = lax.all_gather(master_mask, "tile", axis=0, tiled=True)
    chosen = picker(piece.shape[0])
    placed = jnp.einsum("tr,rxy->txy", chosen, piece.astype(jnp.float32), precision=precise)
    sel_re, sel_im = spectra(placed, cos_tab, sin_tab)
    spec_re = tile_re + (ph_re * sel_re - ph_im * sel_im)
    spec_im = tile_im + (ph_re * sel_im + ph_im * sel_re)
    goal = target.astype(jnp.float32)
    dose = corner_dose[0]
    kern_count = lax.axis_size("kern")
    kern_pos = lax.axis_index("kern")
    per_dev = kernels.shape[1] // kern_count
    first = kern_pos * per_dev
    mine_kern = lax.dynamic_slice_in_dim(kernels[0], first, per_dev, 0)
    kern_re = mine_kern[:, 0]
    kern_im = mine_kern[:, 1]
    weights = lax.dynamic_slice_in_dim(kernel_weight[0], first, per_dev, 0)

    def make_field(h_re, h_im):
        x_re = h_re * spec_re - h_im * spec_im
        x_im = h_re * spec_im + h_im * spec_re
        return to_field(x_re, x_im, cos_tab, sin_tab, scale)

    def forward(total, item):
        h_re, h_im, weight = item
        f_re, f_im = make_field(h_re, h_im)
        return (total + weight * (f_re * f_re + f_im * f_im), None)

    partial_light, unused = lax.scan(
        forward, jnp.zeros((local_tiles, P_SIZE, P_SIZE), jnp.float32), (kern_re, kern_im, weights)
    )
    intensity = lax.psum(partial_light, "kern")
    resist = jax.nn.sigmoid(steepness * (dose * intensity - threshold))
    sens = 2.0 * (resist - goal) * resist * (1.0 - resist) * steepness * dose

    def backward(acc, item):
        h_re, h_im, weight = item
        f_re, f_im = make_field(h_re, h_im)
        g_re = 2.0 * weight * sens * f_re
        g_im = 2.0 * weight * sens * f_im
        x_re, x_im = adjoint(g_re, g_im, cos_tab, sin_tab, scale)
        return ((acc[0] + h_re * x_re + h_im * x_im, acc[1] + h_re * x_im - h_im * x_re), None)

    zero = jnp.zeros((local_tiles, B, B), jnp.float32)
    grads, unused = lax.scan(backward, (zero, zero), (kern_re, kern_im, weights))
    partial_grad = jnp.stack([grads[0], grads[1]], axis=1)
    summed = lax.psum(partial_grad, ("corner", "kern"))
    tile_grad = back_pixels(summed[:, 0], summed[:, 1], cos_tab, sin_tab)
    back_re = ph_re * summed[:, 0] + ph_im * summed[:, 1]
    back_im = ph_re * summed[:, 1] - ph_im * summed[:, 0]
    masters_all = lax.axis_size("tile") * master_mask.shape[0]
    owner_pick = picker(masters_all)
    terms = jnp.stack(
        [
            jnp.einsum("tm,tbc->mbc", owner_pick, back_re, precision=precise),
            jnp.einsum("tm,tbc->mbc", owner_pick, back_im, precision=precise),
        ],
        axis=1,
    )
    mine = lax.psum_scatter(terms, "tile", scatter_dimension=0, tiled=True)
    master_grad = back_pixels(mine[:, 0], mine[:, 1], cos_tab, sin_tab)
    return (tile_grad, master_grad)


def solution(mesh):
    return jax.shard_map(
        on_device,
        mesh=mesh,
        in_specs=(
            P(("region", "tile"), None, None),
            P(("region", "tile"), None, None),
            P(("region", "tile"), None, None),
            P(("region", "tile")),
            P(("region", "tile"), None),
            P("corner", None, None, None, None),
            P("corner", None),
            P("corner"),
        ),
        out_specs=(P(("region", "tile"), None, None), P(("region", "tile"), None, None)),
        check_vma=False,
    )
```

profile of v0, /device:TPU:0, one launch (start us, length us, event | category | flops | bytes accessed | tf_op | source)
XLA Modules:
  0.0 199.7 jit_solution(11332372084410168777)
XLA Ops:
  7.2 17.7 %all_gather.3 = bf16[4,256,256]{2,1,0:T(8,128)(2,1)S(1)} all-gather(bf16[1,256,256]{2,1,0:T(8,128)(2,1)} %param.13), channel_id=1, replica_groups=mesh['region'=2,'tile'=4,'corner'=2,'kern'=2] {'tile'}, dimensions={0}, use_global_device_ids=true | all-gather | bytes 655360 | tf_op jit(solution)/shard_map/all_gather | solution.py:106
  31.6 0.6 copy-done.7
  32.3 37.9 %while.30 = (s32[]{:T(128)}, f32[2,256,256]{2,1,0:T(8,128)S(1)}, f32[6]{0:T(128)S(1)}, f32[6,32,32]{2,1,0:T(8,128)S(1)}, f32[2,32,32]{1,2,0:T(8,128)S(1)}, /*ind...) while((s32[]{:T(128)}, f32[2,256,256]{2,1,0:T(8,128)S(1)}, ...), condition=%wide.region_1.2_spmd.clone.clone.clone.clone, body=%wide.region_0.1_spmd.clone.clone.clone.clone.sunk | while | flops 228810752 | bytes 4981891 | solution.py:133
  33.3 0.8 fusion.461
  34.9 0.8 fusion.464
  35.7 0.8 fusion.465
  37.0 1.6 fusion.466
  39.6 0.8 fusion.461
  41.2 0.8 fusion.464
  42.0 0.8 fusion.465
  43.3 1.6 fusion.466
  46.0 0.8 fusion.461
  47.5 0.8 fusion.464
  48.3 0.8 fusion.465
  49.7 1.6 fusion.466
  52.3 0.8 fusion.461
  53.9 0.8 fusion.464
  54.6 0.8 fusion.465
  56.0 1.6 fusion.466
  58.6 0.8 fusion.461
  60.2 0.8 fusion.464
  61.0 0.8 fusion.465
  62.3 1.6 fusion.466
  64.9 0.8 fusion.461
  66.5 0.8 fusion.464
  67.3 0.8 fusion.465
  68.6 1.6 fusion.466
  70.3 0.8 copy-done.1
  72.0 19.7 %all-reduce.2.cloned.1.call-done = f32[2,256,256]{2,1,0:T(8,128)} async-done(((f32[2,256,256]{2,1,0:T(8,128)}), f32[2,256,256]{2,1,0:T(8,128)}) %all-reduce.2.cloned.1.call-update) | async-done | bytes 524304 | tf_op jit(solution)/shard_map/psum | solution.py:136
  91.7 1.3 multiply_multiply_fusion
  93.0 61.6 %while.31 = (s32[]{:T(128)}, f32[2,32,32]{2,1,0:T(8,128)S(1)}, f32[2,32,32]{2,1,0:T(8,128)S(1)}, f32[6]{0:T(128)S(1)}, f32[2,256,256]{2,1,0:T(8,128)S(1)}, /*ind...) while((s32[]{:T(128)}, f32[2,32,32]{2,1,0:T(8,128)S(1)}, ...), condition=%wide.region_4.5_spmd.clone.clone.clone.clone, body=%wide.region_3.4_spmd.clone.clone.clone.clone.sunk | while | flops 456050688 | bytes 7833771 | solution.py:149
  94.0 0.8 fusion.501
  96.8 0.8 fusion.502
  98.2 0.8 fusion.496
  99.0 0.8 fusion.499
  101.0 0.6 fusion.503
  104.3 0.8 fusion.501
  107.1 0.8 fusion.502
  108.5 0.8 fusion.496
  109.3 0.8 fusion.499
  111.3 0.6 fusion.503
  114.6 0.8 fusion.501
  117.4 0.8 fusion.502
  118.8 0.8 fusion.496
  119.5 0.8 fusion.499
  124.8 0.8 fusion.501
  127.6 0.8 fusion.502
  129.0 0.8 fusion.496
  129.8 0.8 fusion.499
  135.1 0.8 fusion.501
  137.9 0.8 fusion.502
  139.3 0.8 fusion.496
  140.1 0.8 fusion.499
  145.4 0.8 fusion.501
  148.2 0.8 fusion.502
  149.6 0.8 fusion.496
  150.4 0.8 fusion.499
  154.7 12.2 %psum.15 = f32[2,2,32,32]{3,2,0,1:T(8,128)S(1)} all-reduce(f32[2,2,32,32]{3,2,0,1:T(8,128)S(1)} %pad_maximum_fusion.1), channel_id=1, replica_groups=mesh['region'=2,'tile'=4,'corner'=2,'kern'=2] {'corner','kern'}, use_global_device_ids=true, to_apply=%region_5.6 | all-reduce | flops 4096 | bytes 32768 | tf_op jit(solution)/shard_map/psum | solution.py:151
  168.6 0.7 copy.38
  170.1 0.8 fusion.219
  170.9 1.6 convolution_add_fusion.6
  172.5 16.2 %reduce-scatter.2.cloned.1.call-done = f32[1,2,32,32]{3,2,1,0:T(8,128)} async-done(((f32[4,2,32,32]{3,2,1,0:T(8,128)}), f32[1,2,32,32]{3,2,1,0:T(8,128)}) %reduce-scatter.2.cloned.1.call-update) | async-done | bytes 8208 | tf_op jit(solution)/shard_map/reduce_scatter | solution.py:164
  188.7 1.1 fusion.250
  191.6 1.3 fusion.189
  (197 shorter events, 62.4 us)
Async XLA Ops:
  7.2 24.4 %copy-start = (f32[1,12,2,32,32]{4,3,2,1,0:T(8,128)S(1)}, f32[1,12,2,32,32]{4,3,2,1,0:T(8,128)}, u32[]{:S(2)}) copy-start(f32[1,12,2,32,32]{4,3,2,1,0:T(8,128)} %param.17) | copy-start | bytes 294916
  7.2 84.5 %all-reduce.2.cloned.1.call-start = ((), (), s32[]{:S(2)}) async-start(), calls=%async_computation.1 | async-start | bytes 1048576 | tf_op jit(solution)/shard_map/psum | solution.py:136
  7.2 17.7 %copy-start.4 = (s32[2]{0:T(128)S(1)}, s32[2]{0:T(128)}, u32[]{:S(2)}) copy-start(s32[2]{0:T(128)} %param.15) | copy-start | bytes 28
  26.7 1.0 copy-start.2
  29.7 0.7 copy-start.5
  31.6 0.7 copy-start.7
  70.3 0.8 copy-start.1
  70.3 21.4 %copy-start.3 = (bf16[2,256,256]{2,1,0:T(8,128)(2,1)S(1)}, bf16[2,256,256]{2,1,0:T(8,128)(2,1)}, u32[]{:S(2)}) copy-start(bf16[2,256,256]{2,1,0:T(8,128)(2,1)} %param.14) | copy-start | bytes 786436
  71.1 117.6 %reduce-scatter.2.cloned.1.call-start = ((), (), s32[]{:S(2)}) async-start(), calls=%async_computation.2 | async-start | bytes 163840 | tf_op jit(solution)/shard_map/reduce_scatter | solution.py:164
  188.7 1.2 copy-start.6
Sparse Core Ops, SparseCore 0:
  71.2 20.4 all-reduce.1
  169.5 19.2 reduce-scatter.1
where the time goes:
time: 200 us
  matrix products  99.7 us (50%)
  waiting for transfers between devices  36 us (18%)
  blocking collectives  29.9 us (15%)
  between operations  15 us (8%)
  local copies, waits for them, and re-layouts  11.7 us (6%)
  loops' own time  5.29 us (3%)
    psum x1, waiting for transfers between devices, on_device(): intensity = lax.psum(partial_light, 'kern')  19.7 us
    all_gather x1, blocking collectives, on_device(): piece = lax.all_gather(master_mask, 'tile', axis=0, tiled=True)  17.7 us
    reduce_scatter x1, waiting for transfers between devices, on_device(): mine = lax.psum_scatter(terms, 'tile', scatter_dimension=0, tiled=True)  16.2 us
    dot_general x12, matrix products, to_field(): jnp.einsum('nxc,cy->nxy', half_im, sin_tab, precision=precise)  14.3 us
    psum x1, blocking collectives, on_device(): summed = lax.psum(partial_grad, ('corner', 'kern'))  12.2 us
    dot_general x12, matrix products, to_field(): jnp.einsum('nxc,cy->nxy', half_re, sin_tab, precision=precise)  9.2 us
    dot_general x12, matrix products, to_field(): jnp.einsum('nxc,cy->nxy', half_im, cos_tab, precision=precise)  9.12 us
    dot_general x12, matrix products, to_field(): jnp.einsum('nxc,cy->nxy', half_re, cos_tab, precision=precise)  9.1 us
  transfers between devices with their start and end apart: 2, of which 2 were waited for; matrix products, arithmetic and copies ran while one was open for 2% of the time, Pallas kernels for 0%

commit v1 on v0

--- a/solution.py
+++ b/solution.py
@@ -9,6 +9,24 @@
 precise = lax.Precision.HIGHEST
 steepness = 3.0
 threshold = 1.0
+
+
+def ring_gather(array, axis, dim):
+    ways, here, lap = (lax.axis_size(axis), lax.axis_index(axis), array.shape[dim])
+    shape = [n * ways if d == dim else n for d, n in enumerate(array.shape)]
+    full = lax.dynamic_update_slice_in_dim(
+        jnp.zeros(shape, array.dtype), array, here * lap, axis=dim
+    )
+    going_up = going_down = array
+    for far in range(1, ways // 2 + 1):
+        going_up = lax.ppermute(going_up, axis, [(d, (d + 1) % ways) for d in range(ways)])
+        full = lax.dynamic_update_slice_in_dim(full, going_up, (here - far) % ways * lap, axis=dim)
+        if 2 * far < ways:
+            going_down = lax.ppermute(going_down, axis, [(d, (d - 1) % ways) for d in range(ways)])
+            full = lax.dynamic_update_slice_in_dim(
+                full, going_down, (here + far) % ways * lap, axis=dim
+            )
+    return full
 
 
 def band_tables():
@@ -103,7 +121,7 @@
         index = jnp.arange(count, dtype=jnp.int32)
         return (inst_master[:, None] == index[None, :]).astype(jnp.float32)
 
-    piece = lax.all_gather(master_mask, "tile", axis=0, tiled=True)
+    piece = ring_gather(master_mask, "tile", 0)
     chosen = picker(piece.shape[0])
     placed = jnp.einsum("tr,rxy->txy", chosen, piece.astype(jnp.float32), precision=precise)
     sel_re, sel_im = spectra(placed, cos_tab, sin_tab)

time: 200 us -> 204 us (1.020)
  blocking collectives: 29.9 us -> 12.2 us
  local copies, waits for them, and re-layouts: 11.7 us -> 25.4 us
  starting transfers between devices: 0.26 us -> 5.43 us
    all_gather x1 -> x0, blocking collectives: 17.7 us -> none  [on_device(): piece = lax.all_gather(master_mask, 'tile', axis=0, tiled=True)]
    dynamic_update_slice x0 -> x4, local copies, waits for them, and re-layouts: none -> 13.5 us  [the longest x2 6.75 us: ring_gather(): lax.dynamic_update_slice_in_dim(full, going_up, (here - far) % ways * lap...]
    ppermute x0 -> x3, starting transfers between devices: none -> 5.17 us  [the longest x2 3.08 us: ring_gather(): lax.ppermute(going_up, axis, [(d, (d + 1) % ways) for d in range(ways)])]
  transfers between devices with their start and end apart: 2 -> 5, of which waited for: 2 -> 3; matrix products, arithmetic and copies ran while one was open for 2% -> 8% of each run, Pallas kernels for 0% -> 0%
where the time goes in v1:
time: 204 us; the launch traced here: 203 us
  matrix products  101 us (50%)
  waiting for transfers between devices  37.4 us (18%)
  local copies, waits for them, and re-layouts  25.4 us (12%)
  between operations  15.2 us (7%)
  blocking collectives  12.2 us (6%)
  starting transfers between devices  5.43 us (3%)
  loops' own time  5.29 us (3%)
    psum x1, waiting for transfers between devices, on_device(): intensity = lax.psum(partial_light, 'kern')  19.7 us
    reduce_scatter x1, waiting for transfers between devices, on_device(): mine = lax.psum_scatter(terms, 'tile', scatter_dimension=0, tiled=True)  16.3 us
    dot_general x12, matrix products, to_field(): jnp.einsum('nxc,cy->nxy', half_im, sin_tab, precision=precise)  14.4 us
    psum x1, blocking collectives, on_device(): summed = lax.psum(partial_grad, ('corner', 'kern'))  12.2 us
    dot_general x12, matrix products, to_field(): jnp.einsum('nxc,cy->nxy', half_re, sin_tab, precision=precise)  9.21 us
    dot_general x12, matrix products, to_field(): jnp.einsum('nxc,cy->nxy', half_re, cos_tab, precision=precise)  9.12 us
    dot_general x12, matrix products, to_field(): jnp.einsum('nxc,cy->nxy', half_im, cos_tab, precision=precise)  9.12 us
    dynamic_slice x30, local copies, waits for them, and re-layouts, on_device(): lax.scan(forward, jnp.zeros((local_tiles, P_SIZE, P_SIZE), jnp.float32),...  7.97 us
  transfers between devices with their start and end apart: 5, of which 3 were waited for; matrix products, arithmetic and copies ran while one was open for 8% of the time, Pallas kernels for 0%

profile of v1, /device:TPU:0, one launch (start us, length us, event | category | flops | bytes accessed | tf_op | source)
XLA Modules:
  0.0 203.3 jit_solution(12753898354974016477)
XLA Ops:
  7.2 3.1 %collective-permute-start = (bf16[1,256,256]{2,1,0:T(8,128)(2,1)}, bf16[1,256,256]{2,1,0:T(8,128)(2,1)S(1)}, u32[]{:S(2)}, u32[]{:S(2)}) collective-permute-start(bf16[1,256,256]{2,1,0:T(8,128)(2,1)} %param.13), channel_id=1, source_target_pairs={{0,4},{4,8},{8,12},{12,0},{1,5},{5,9},{9,13},{13,1},{2,6},{6,10},{... | collective-permute-start | bytes 393224 | tf_op jit(solution)/shard_map/ppermute | solution.py:22
  10.3 2.1 %collective-permute-start.1 = (bf16[1,256,256]{2,1,0:T(8,128)(2,1)}, bf16[1,256,256]{2,1,0:T(8,128)(2,1)S(1)}, u32[]{:S(2)}, u32[]{:S(2)}) collective-permute-start(bf16[1,256,256]{2,1,0:T(8,128)(2,1)} %param.13), channel_id=1, source_target_pairs={{0,12},{4,0},{8,4},{12,8},{1,13},{5,1},{9,5},{13,9},{2,14},{6,2},{... | collective-permute-start | bytes 393224 | tf_op jit(solution)/shard_map/ppermute | solution.py:25
  12.4 1.3 convolution_bitcast_fusion.3
  15.5 1.4 collective-permute-done
  17.4 3.4 %dynamic_update_slice.12 = bf16[4,256,256]{2,0,1:T(4,128)(2,1)S(1)} dynamic-update-slice(bf16[4,256,256]{2,0,1:T(4,128)(2,1)S(1)} %broadcast_in_dim.8, bf16[1,256,256]{2,0,1:T(2,128)(2,1)S(1)} %copy.30, s32[]{:T(128)S(6)} %select_n.140, s32[]{:T(128)} %constant.87.clone.1, s32[]{:T(128)} %constant.87.clone.1) | dynamic-update-slice | bytes 262148 | tf_op jit(solution)/shard_map/dynamic_update_slice | solution.py:17
  21.1 3.4 %dynamic_update_slice.13 = bf16[4,256,256]{2,0,1:T(4,128)(2,1)S(1)} dynamic-update-slice(bf16[4,256,256]{2,0,1:T(4,128)(2,1)S(1)} %dynamic_update_slice.12, bf16[1,256,256]{2,0,1:T(2,128)(2,1)S(1)} %copy.31, s32[]{:T(128)S(6)} %select_n.142, s32[]{:T(128)} %constant.87.clone.1, s32[]{:T(128)} %constant.87.clone.1) | dynamic-update-slice | bytes 262148 | tf_op jit(solution)/shard_map/dynamic_update_slice | solution.py:23
  24.7 3.4 %dynamic_update_slice.14 = bf16[4,256,256]{2,0,1:T(4,128)(2,1)S(1)} dynamic-update-slice(bf16[4,256,256]{2,0,1:T(4,128)(2,1)S(1)} %dynamic_update_slice.13, bf16[1,256,256]{2,0,1:T(2,128)(2,1)S(1)} %copy.32, s32[]{:T(128)S(6)} %select_n.144, s32[]{:T(128)} %constant.87.clone.1, s32[]{:T(128)} %constant.87.clone.1) | dynamic-update-slice | bytes 262148 | tf_op jit(solution)/shard_map/dynamic_update_slice | solution.py:26
  28.3 3.4 %dynamic_update_slice.15 = bf16[4,256,256]{2,0,1:T(4,128)(2,1)S(1)} dynamic-update-slice(bf16[4,256,256]{2,0,1:T(4,128)(2,1)S(1)} %dynamic_update_slice.14, bf16[1,256,256]{2,0,1:T(2,128)(2,1)S(1)} %copy.33, s32[]{:T(128)S(6)} %select_n.146, s32[]{:T(128)} %constant.87.clone.1, s32[]{:T(128)} %constant.87.clone.1) | dynamic-update-slice | bytes 262148 | tf_op jit(solution)/shard_map/dynamic_update_slice | solution.py:23
  36.0 38.0 %while.30 = (s32[]{:T(128)}, f32[2,256,256]{2,1,0:T(8,128)S(1)}, f32[6]{0:T(128)S(1)}, f32[6,32,32]{2,1,0:T(8,128)S(1)}, f32[2,32,32]{1,2,0:T(8,128)S(1)}, /*ind...) while((s32[]{:T(128)}, f32[2,256,256]{2,1,0:T(8,128)S(1)}, ...), condition=%wide.region_1.2_spmd.clone.clone.clone.clone, body=%wide.region_0.1_spmd.clone.clone.clone.clone.sunk | while | flops 228810752 | bytes 4981891 | solution.py:151
  37.0 0.8 fusion.461
  38.5 0.8 fusion.464
  39.3 0.8 fusion.465
  40.7 1.6 fusion.466
  43.3 0.8 fusion.461
  44.9 0.8 fusion.464
  45.6 0.8 fusion.465
  47.0 1.6 fusion.466
  49.6 0.8 fusion.461
  51.2 0.8 fusion.464
  52.0 0.8 fusion.465
  53.3 1.6 fusion.466
  56.0 0.8 fusion.461
  57.5 0.8 fusion.464
  58.3 0.8 fusion.465
  59.7 1.6 fusion.466
  62.3 0.8 fusion.461
  63.9 0.8 fusion.464
  64.6 0.8 fusion.465
  66.0 1.6 fusion.466
  68.6 0.8 fusion.461
  70.2 0.8 fusion.464
  71.0 0.8 fusion.465
  72.3 1.6 fusion.466
  74.0 0.8 copy-done.1
  75.7 19.7 %all-reduce.2.cloned.1.call-done = f32[2,256,256]{2,1,0:T(8,128)} async-done(((f32[2,256,256]{2,1,0:T(8,128)}), f32[2,256,256]{2,1,0:T(8,128)}) %all-reduce.2.cloned.1.call-update) | async-done | bytes 524304 | tf_op jit(solution)/shard_map/psum | solution.py:154
  95.4 1.3 multiply_multiply_fusion
  96.7 61.6 %while.31 = (s32[]{:T(128)}, f32[2,32,32]{2,1,0:T(8,128)S(1)}, f32[2,32,32]{2,1,0:T(8,128)S(1)}, f32[6]{0:T(128)S(1)}, f32[2,256,256]{2,1,0:T(8,128)S(1)}, /*ind...) while((s32[]{:T(128)}, f32[2,32,32]{2,1,0:T(8,128)S(1)}, ...), condition=%wide.region_4.5_spmd.clone.clone.clone.clone, body=%wide.region_3.4_spmd.clone.clone.clone.clone.sunk | while | flops 456050688 | bytes 7833771 | solution.py:167
  97.7 0.8 fusion.501
  100.5 0.8 fusion.502
  101.9 0.8 fusion.496
  102.6 0.8 fusion.499
  107.9 0.8 fusion.501
  110.8 0.8 fusion.502
  112.2 0.8 fusion.496
  112.9 0.8 fusion.499
  121.0 0.8 fusion.502
  122.4 0.8 fusion.496
  123.2 0.8 fusion.499
  131.3 0.8 fusion.502
  132.7 0.8 fusion.496
  133.5 0.8 fusion.499
  138.8 0.8 fusion.501
  141.6 0.8 fusion.502
  143.0 0.8 fusion.496
  143.7 0.8 fusion.499
  151.8 0.8 fusion.502
  153.2 0.8 fusion.496
  154.0 0.8 fusion.499
  158.3 12.2 %psum.15 = f32[2,2,32,32]{3,2,0,1:T(8,128)S(1)} all-reduce(f32[2,2,32,32]{3,2,0,1:T(8,128)S(1)} %pad_maximum_fusion.1), channel_id=1, replica_groups=mesh['region'=2,'tile'=4,'corner'=2,'kern'=2] {'corner','kern'}, use_global_device_ids=true, to_apply=%region_5.6 | all-reduce | flops 4096 | bytes 32768 | tf_op jit(solution)/shard_map/psum | solution.py:169
  173.8 0.8 fusion.217
  174.6 1.6 convolution_add_fusion.6
  176.1 16.3 %reduce-scatter.2.cloned.1.call-done = f32[1,2,32,32]{3,2,1,0:T(8,128)} async-done(((f32[4,2,32,32]{3,2,1,0:T(8,128)}), f32[1,2,32,32]{3,2,1,0:T(8,128)}) %reduce-scatter.2.cloned.1.call-update) | async-done | bytes 8208 | tf_op jit(solution)/shard_map/reduce_scatter | solution.py:182
  192.4 1.1 fusion.248
  195.2 1.3 fusion.189
  (213 shorter events, 66.9 us)
Async XLA Ops:
  7.2 7.4 %copy-start = (f32[1,12,2,32,32]{4,3,2,1,0:T(8,128)S(1)}, f32[1,12,2,32,32]{4,3,2,1,0:T(8,128)}, u32[]{:S(2)}) copy-start(f32[1,12,2,32,32]{4,3,2,1,0:T(8,128)} %param.17) | copy-start | bytes 294916
  7.2 6.6 %copy-start.2 = (bf16[2,256,256]{2,1,0:T(8,128)(2,1)S(1)}, bf16[2,256,256]{2,1,0:T(8,128)(2,1)}, u32[]{:S(2)}) copy-start(bf16[2,256,256]{2,1,0:T(8,128)(2,1)} %param.12) | copy-start | bytes 786436
  7.2 88.2 %all-reduce.2.cloned.1.call-start = ((), (), s32[]{:S(2)}) async-start(), calls=%async_computation.1 | async-start | bytes 1048576 | tf_op jit(solution)/shard_map/psum | solution.py:154
  7.2 9.6 %collective-permute-start = (bf16[1,256,256]{2,1,0:T(8,128)(2,1)}, bf16[1,256,256]{2,1,0:T(8,128)(2,1)S(1)}, u32[]{:S(2)}, u32[]{:S(2)}) collective-permute-start(bf16[1,256,256]{2,1,0:T(8,128)(2,1)} %param.13), channel_id=1, source_target_pairs={{0,4},{4,8},{8,12},{12,0},{1,5},{5,9},{9,13},{13,1},{2,6},{6,10},{... | collective-permute-start | bytes 393224 | tf_op jit(solution)/shard_map/ppermute | solution.py:22
  10.3 14.1 %collective-permute-start.1 = (bf16[1,256,256]{2,1,0:T(8,128)(2,1)}, bf16[1,256,256]{2,1,0:T(8,128)(2,1)S(1)}, u32[]{:S(2)}, u32[]{:S(2)}) collective-permute-start(bf16[1,256,256]{2,1,0:T(8,128)(2,1)} %param.13), channel_id=1, source_target_pairs={{0,12},{4,0},{8,4},{12,8},{1,13},{5,1},{9,5},{13,9},{2,14},{6,2},{... | collective-permute-start | bytes 393224 | tf_op jit(solution)/shard_map/ppermute | solution.py:25
  14.6 0.7 copy-start.6
  14.6 2.4 %copy-start.4 = (bf16[1,256,256]{2,1,0:T(8,128)(2,1)S(1)}, bf16[1,256,256]{2,1,0:T(8,128)(2,1)}, u32[]{:S(2)}) copy-start(bf16[1,256,256]{2,1,0:T(8,128)(2,1)} %param.13) | copy-start | bytes 393220
  16.9 11.2 %collective-permute-start.2 = (bf16[1,256,256]{2,1,0:T(8,128)(2,1)S(1)}, bf16[1,256,256]{2,1,0:T(8,128)(2,1)S(1)}, u32[]{:S(2)}, u32[]{:S(2)}) collective-permute-start(bf16[1,256,256]{2,1,0:T(8,128)(2,1)S(1)} %collective-permute-done), channel_id=1, source_target_pairs={{0,4},{4,8},{8,12},{12,0},{1,5},{5,9},{9,13},{13,1},{2,6},{6,10},{... | collective-permute-start | bytes 393224 | tf_op jit(solution)/shard_map/ppermute | solution.py:22
  17.4 3.4 %copy-start.8 = (f32[1,12]{1,0:T(1,128)S(1)}, f32[1,12]{1,0:T(1,128)}, u32[]{:S(2)}) copy-start(f32[1,12]{1,0:T(1,128)} %param.18) | copy-start | bytes 148
  28.3 3.4 %copy-start.5 = (s32[2]{0:T(128)S(1)}, s32[2]{0:T(128)}, u32[]{:S(2)}) copy-start(s32[2]{0:T(128)} %param.15) | copy-start | bytes 28
  74.0 0.8 copy-start.1
  74.0 21.4 %copy-start.3 = (bf16[2,256,256]{2,1,0:T(8,128)(2,1)S(1)}, bf16[2,256,256]{2,1,0:T(8,128)(2,1)}, u32[]{:S(2)}) copy-start(bf16[2,256,256]{2,1,0:T(8,128)(2,1)} %param.14) | copy-start | bytes 786436
  74.8 117.6 %reduce-scatter.2.cloned.1.call-start = ((), (), s32[]{:S(2)}) async-start(), calls=%async_computation.2 | async-start | bytes 163840 | tf_op jit(solution)/shard_map/reduce_scatter | solution.py:182
  192.4 1.2 copy-start.7
Sparse Core Ops, SparseCore 0:
  74.9 20.4 all-reduce.1
  173.1 19.2 reduce-scatter.1
